TPU v7x, 32 devices: a whole 2x2x4 slice. The times are simulated.
32 devices in a mesh: groups: 2 (over y), ctx: 4 (over z), chan: 2 (over x), sub: 2 (over core).
Axes of the slice: x: 2, y: 2, z: 4, core: 2. Of those that a mesh axis runs over, the one named last changes fastest.
Arguments:
- queries: float32 [2048, 8192], P(('groups', 'ctx'), ('chan', 'sub')), parts along dimension 0, may hold values from -6 to 6
- key_in: float32 [2048, 8192], P(('groups', 'ctx'), ('chan', 'sub')), parts along dimension 0, may hold values from -6 to 6
- values_in: float32 [2048, 8192], P(('groups', 'ctx'), ('chan', 'sub')), parts along dimension 0, may hold values from -6 to 6
- skip_gain: float32 [8192], P(('chan', 'sub')), may hold values from 0.5 to 1.5
- filter_tap_bank: float32 [16, 256, 512], P(('ctx', 'sub'), None, 'chan'), may hold values from -0.1875 to 0.1875
- lag_slot: int32 [4], replicated, may hold values from 0 to 15, as said below
Outputs:
- gated_output: float32 [2048, 8192], P(('groups', 'ctx'), ('chan', 'sub')), parts along dimension 0
There are 2 independent parts, one for each index of `groups`. A program takes and returns all parts, laid end to end along the dimension named above; an argument that names none is the same for every part. Nothing has to cross between parts.
Inputs may be any that keep to these rules, and one draw needn't show every extreme that they name: `lag_slot`: the 4 entries are distinct slots; entry k names the slot that holds lags k * 256 to (k + 1) * 256 - 1.
All inputs are finite; a program needn't handle non-finite values.
Results may differ from a plain program's by a relative error of at most 0.00005.
Values sent between devices are 32-bit elements; how exact they have to be, the bound alone decides.
No kernel may reach another device: no remote copies, remote signals or barrier semaphores. Data moves between devices by JAX's collectives and lax.ppermute only.
A program may use at most 128 MiB of HBM per device.

v0:
```python
import jax
import jax.numpy as jnp
from jax import lax
from jax.sharding import PartitionSpec as P

HIGHEST = lax.Precision.HIGHEST
DATA_PRECISION = lax.Precision.HIGH
CHUNKS = 4


def from_root(block, axis, owner):
    block = jnp.where(lax.axis_index(axis) == owner, block, jnp.zeros_like(block))
    return lax.psum(block, axis)


def tables(length):
    freq_rows = lax.broadcasted_iota(jnp.int32, (length, length), 0)
    place_cols = lax.broadcasted_iota(jnp.int32, (length, length), 1)
    angle = jnp.pi * (freq_rows * place_cols % (2 * length)).astype(jnp.float32) / length
    parity = 1.0 - 2.0 * (place_cols % 2).astype(jnp.float32)
    fwd_real = jnp.cos(angle)
    fwd_imag = jnp.where(freq_rows == 0, parity, -jnp.sin(angle))
    out_place = freq_rows + length
    back_angle = jnp.pi * (place_cols * out_place % (2 * length)).astype(jnp.float32) / length
    out_parity = 1.0 - 2.0 * (out_place % 2).astype(jnp.float32)
    inv_real = jnp.where(place_cols == 0, 1.0, 2.0 * jnp.cos(back_angle)) / (2 * length)
    inv_imag = jnp.where(place_cols == 0, out_parity, -2.0 * jnp.sin(back_angle)) / (2 * length)
    return (fwd_real, fwd_imag, inv_real, inv_imag)


def transform(block, fwd_real, fwd_imag, precision=DATA_PRECISION):
    return jnp.stack(
        [jnp.dot(fwd_real, block, precision=precision), jnp.dot(fwd_imag, block, precision=precision)]
    )


def transform_rows(block, fwd_real, fwd_imag):
    return jnp.stack(
        [
            jnp.einsum("pc,fp->cf", block, fwd_real, precision=DATA_PRECISION),
            jnp.einsum("pc,fp->cf", block, fwd_imag, precision=DATA_PRECISION),
        ]
    )


def inverse_rows(total, inv_real, inv_imag):
    return jnp.einsum("tf,cf->tc", inv_real, total[0], precision=DATA_PRECISION) + jnp.einsum(
        "tf,cf->tc", inv_imag, total[1], precision=DATA_PRECISION
    )


def apply_filter(spectrum, filt):
    chan_width = spectrum.shape[1]
    length = spectrum.shape[2]
    group_dev = filt.shape[1]
    a_real = spectrum[0].reshape(group_dev, chan_width // group_dev, length)
    a_imag = spectrum[1].reshape(group_dev, chan_width // group_dev, length)
    e_real = filt[0][:, None, :]
    e_imag = filt[1][:, None, :]
    first_col = lax.broadcasted_iota(jnp.int32, (1, 1, length), 2) == 0
    prod_real = jnp.where(first_col, a_real * e_real, a_real * e_real - a_imag * e_imag)
    prod_imag = jnp.where(first_col, a_imag * e_imag, a_real * e_imag + a_imag * e_real)
    return jnp.stack([prod_real.reshape(chan_width, length), prod_imag.reshape(chan_width, length)])


def filtered_sum(specs, filters):
    total = apply_filter(specs[0], filters[0])
    for spec, filt in zip(specs[1:], filters[1:]):
        total = total + apply_filter(spec, filt)
    return total


def body(queries, key_in, values_in, skip_gain, filter_tap_bank, lag_slot):
    length, chan_width = key_in.shape
    slots_dev = filter_tap_bank.shape[0]
    cycle_steps = lag_slot.shape[0]
    group_dev = filter_tap_bank.shape[2] // lax.axis_size("sub")
    n_ctx = lax.axis_size("ctx")
    sub_index = lax.axis_index("sub")
    mixed_input = key_in * values_in
    fwd_real, fwd_imag, inv_real, inv_imag = lax.optimization_barrier(tables(length))
    members = chan_width // group_dev
    n_sub = lax.axis_size("sub")
    received = []
    for offset in range(n_sub):
        wanted = lax.dynamic_slice_in_dim(
            filter_tap_bank, ((sub_index + offset) % n_sub) * group_dev, group_dev, 2
        )
        if offset:
            wanted = lax.ppermute(
                wanted, "sub", [(i, (i + offset) % n_sub) for i in range(n_sub)]
            )
        received.append(wanted)
    received = jnp.stack(received)
    pieces = []
    for cycle_step in range(cycle_steps):
        slot_index = lag_slot[cycle_step]
        owner = slot_index // slots_dev
        source = (sub_index - owner % n_sub) % n_sub
        held_piece = received[source, slot_index % slots_dev]
        pieces.append(from_root(held_piece, "ctx", owner // n_sub))
    filter_taps = jnp.concatenate(pieces, axis=1)
    filter_spec = jnp.stack(
        [
            jnp.einsum("pk,fp->kf", filter_taps, fwd_real, precision=HIGHEST),
            jnp.einsum("pk,fp->kf", filter_taps, fwd_imag, precision=HIGHEST),
        ]
    )
    col_sign = (
        1.0 - 2.0 * (lax.broadcasted_iota(jnp.int32, (1, length), 1) % 2).astype(jnp.float32)
    )[None]
    segment_spec = [
        filter_spec[:, cycle_step * group_dev : (cycle_step + 1) * group_dev]
        for cycle_step in range(cycle_steps)
    ]
    effective = [col_sign * segment_spec[0]]
    for cycle_step in range(1, cycle_steps):
        effective.append(segment_spec[cycle_step - 1] + col_sign * segment_spec[cycle_step])
    effective.append(segment_spec[cycle_steps - 1])

    last_raw = max(n_ctx - 2, 0)
    raw_rounds = min(cycle_steps, last_raw)
    part_terms = min(cycle_steps, raw_rounds + 1)
    chunks = CHUNKS if group_dev % CHUNKS == 0 else 1
    chunk_w = chan_width // chunks
    chunk_g = group_dev // chunks
    first_round = None
    if raw_rounds:
        first_round = lax.ppermute(mixed_input, "ctx", [(k, k + 1) for k in range(0, last_raw)])
    outs = []
    last_round = None
    partial = None
    sent = None
    for chunk in range(chunks):
        cols = slice(chunk * chunk_w, (chunk + 1) * chunk_w)
        filters = [e[:, chunk * chunk_g : (chunk + 1) * chunk_g] for e in effective]
        moving = mixed_input[:, cols]
        blocks = [moving]
        for step in range(1, raw_rounds + 1):
            route = [(k, k + 1) for k in range(step - 1, last_raw)]
            if step == raw_rounds and step > 1 and last_round is not None:
                moving, _ = lax.optimization_barrier((moving, last_round))
            if step == 1:
                moving = first_round[:, cols]
            else:
                moving = lax.ppermute(moving, "ctx", route)
            if step == raw_rounds and step > 1 and partial is not None:
                moving, _ = lax.optimization_barrier((moving, partial))
            blocks.append(moving)
        if raw_rounds > 1:
            last_round = blocks[-1]
        specs = [transform_rows(b, fwd_real, fwd_imag) for b in blocks]
        conv_out = inverse_rows(filtered_sum(specs, filters), inv_real, inv_imag)
        if n_ctx >= 2:
            part_specs = specs[:part_terms]
            if sent is not None:
                part_specs, _ = lax.optimization_barrier((part_specs, sent))
            partial = inverse_rows(
                filtered_sum(part_specs, filters[1 : part_terms + 1]), inv_real, inv_imag
            )
            sent = lax.ppermute(partial, "ctx", [(last_raw, last_raw + 1)])
            conv_out = conv_out + sent
        outs.append(conv_out)
    conv_all = jnp.concatenate(outs, axis=1) if chunks > 1 else outs[0]
    return queries * (conv_all + skip_gain[None, :] * mixed_input)


def solution(mesh):
    in_specs = (
        P(("groups", "ctx"), ("chan", "sub")),
        P(("groups", "ctx"), ("chan", "sub")),
        P(("groups", "ctx"), ("chan", "sub")),
        P(("chan", "sub")),
        P(("ctx", "sub"), None, "chan"),
        P(),
    )
    out_specs = P(("groups", "ctx"), ("chan", "sub"))
    return jax.shard_map(body, mesh=mesh, in_specs=in_specs, out_specs=out_specs, check_vma=False)
```

profile of v0, /device:TPU:24, one launch (start us, length us, event | category | flops | bytes accessed | tf_op | source)
XLA Modules:
  0.0 181.5 jit_solution(9966554393678137026)
XLA Ops:
  6.5 1.8 constant_dynamic-slice_fusion
  8.3 2.6 %mul.1268 = f32[256,2048]{1,0:T(8,128)S(1)} multiply(f32[256,2048]{1,0:T(8,128)} %param.7, f32[256,2048]{1,0:T(8,128)} %param.8) | non-fusion elementwise | flops 524288 | bytes 6291456 | tf_op jit(solution)/shard_map/mul | solution.py:80
  10.9 2.0 %collective-permute-start.1 = (f32[256,2048]{1,0:T(8,128)S(1)}, f32[256,2048]{1,0:T(8,128)}, u32[]{:S(2)}, u32[]{:S(2)}) collective-permute-start(f32[256,2048]{1,0:T(8,128)S(1)} %mul.1268), channel_id=1, source_target_pairs={{0,4},{4,8},{1,5},{5,9},{2,6},{6,10},{3,7},{7,11},{16,20},{20,24},... | collective-permute-start | bytes 6291464 | tf_op jit(solution)/shard_map/ppermute | solution.py:129
  23.6 1.0 fusion.129
  24.6 2.1 %select_multiply_fusion = (f32[256,256]{1,0:T(8,128)S(1)}, f32[256,256]{1,0:T(8,128)S(1)}, f32[256,256]{1,0:T(8,128)S(1)}) fusion(s32[256]{0:T(256)S(1)} %get-tuple-element.187, s32[256]{0:T(256)S(1)} %get-tuple-element.188, s32[256]{0:T(256)S(1)} %get-tuple-element.191, pred[256]{0:T(512)(128)(4,1)S(1)} %get-tuple-element.189, ...), kind=kLoop, calls=%fused_computation.299 | loop fusion | flops 2883584 | bytes 792320 | tf_op jit(solution)/shard_map/div | solution.py:27
  27.3 1.4 fusion.96
  29.4 1.4 fusion.98
  30.8 1.4 fusion.88
  32.2 1.4 fusion.90
  33.7 1.0 pad_maximum_fusion
  34.7 1.4 fusion.84
  36.1 0.7 fusion.128
  36.8 1.8 %fusion.119 = (f32[256,128]{1,0:T(8,128)}, f32[256,128]{1,0:T(8,128)}, f32[256,128]{1,0:T(8,128)}) fusion(s32[]{:T(128)S(6)} %select_n.533, s32[]{:T(128)S(6)} %select_n.535, f32[1,2,256,128]{3,2,1,0:T(8,128)S(1)} %get-tuple-element.113, f32[1,2,256,128]{3,2,1,0:T(8,128)} %bitcast.2, pred[]{:T(512)S(6)} %eq.174, s32[]{:T(128)S(6)} %select_n.503, ...), kind=kLoop, calls=%fused_computation.310 | loop fusion | flops 196608 | bytes 917531 | tf_op jit(solution)/shard_map/jit(_where)/select_n | solution.py:12
  38.7 2.3 %pad_maximum_fusion.3 = f32[2,512,256]{2,1,0:T(8,128)} fusion(f32[1,512,256]{2,1,0:T(8,128)} %bitcast.680, f32[1,512,256]{2,1,0:T(8,128)} %bitcast.681), kind=kLoop, calls=%fused_computation.51 | loop fusion | flops 262144 | bytes 2097152 | tf_op jit(solution)/shard_map/stack | solution.py:38
  41.6 0.8 copy-done.8
  42.4 1.0 pad_maximum_fusion.6
  43.5 38.9 %all-reduce.3.cloned.1.call-done = (f32[256,128]{1,0:T(8,128)}, f32[256,128]{1,0:T(8,128)}, f32[256,128]{1,0:T(8,128)}, f32[256,128]{1,0:T(8,128)}) async-done(((f32[256,128]{1,0:T(8,128)}, f32[256,128]{1,0:T(8,128)}, f32[256,128]{1,0:T(8,128)}, f32[256,128]{1,0:T(8,128)}), (f32[256,128]{1,0:T(8,128)}, f32[256,128]{1,0:T(8,128)}, f32[256,128]{1,0:T(8,128)}, ...) | async-done | bytes 524304 | tf_op jit(solution)/shard_map/psum | solution.py:13
  82.4 0.9 constant_dynamic-update-slice_fusion.3
  83.3 0.9 constant_dynamic-update-slice_fusion.2
  84.3 0.9 constant_dynamic-update-slice_fusion.1
  85.2 0.9 constant_dynamic-update-slice_fusion
  86.1 1.0 convolution_bitcast_fusion.1
  87.1 1.0 convolution_bitcast_fusion
  88.4 1.7 fusion.148
  90.1 0.9 collective-permute-start.2
  91.0 1.7 fusion.140
  92.7 1.7 fusion.142
  94.4 1.7 fusion.136
  96.1 1.7 fusion.138
  97.8 1.7 fusion.132
  99.5 1.7 fusion.134
  101.2 1.7 fusion.144
  102.9 1.8 fusion.146
  104.7 0.7 collective-permute-start.4
  106.7 1.0 fusion.13
  108.8 1.3 collective-permute-start.3
  112.1 11.0 %collective-permute-done.3 = f32[256,512]{1,0:T(8,128)S(1)} collective-permute-done((f32[256,512]{1,0:T(8,128)S(1)}, f32[256,512]{1,0:T(8,128)S(1)}, u32[]{:S(2)}, u32[]{:S(2)}) %collective-permute-start.3) | collective-permute-done | bytes 524320 | tf_op jit(solution)/shard_map/ppermute | solution.py:161
  124.9 1.3 collective-permute-start.5
  126.2 0.9 collective-permute-start.6
  127.2 0.7 fusion.21
  130.3 8.1 %collective-permute-done.5 = f32[256,512]{1,0:T(8,128)S(1)} collective-permute-done((f32[256,512]{1,0:T(8,128)S(1)}, f32[256,512]{1,0:T(8,128)S(1)}, u32[]{:S(2)}, u32[]{:S(2)}) %collective-permute-start.5) | collective-permute-done | bytes 524320 | tf_op jit(solution)/shard_map/ppermute | solution.py:161
  139.9 0.7 collective-permute-start.8
  141.0 1.4 collective-permute-start.7
  144.2 0.7 fusion.24
  145.6 12.1 %collective-permute-done.7 = f32[256,512]{1,0:T(8,128)S(1)} collective-permute-done((f32[256,512]{1,0:T(8,128)S(1)}, f32[256,512]{1,0:T(8,128)S(1)}, u32[]{:S(2)}, u32[]{:S(2)}) %collective-permute-start.7) | collective-permute-done | bytes 524320 | tf_op jit(solution)/shard_map/ppermute | solution.py:161
  159.5 1.3 collective-permute-start.9
  161.9 10.4 %collective-permute-done.9 = f32[256,512]{1,0:T(8,128)S(1)} collective-permute-done((f32[256,512]{1,0:T(8,128)S(1)}, f32[256,512]{1,0:T(8,128)S(1)}, u32[]{:S(2)}, u32[]{:S(2)}) %collective-permute-start.9) | collective-permute-done | bytes 524320 | tf_op jit(solution)/shard_map/ppermute | solution.py:161
  172.7 1.9 %fusion = f32[256,2048]{1,0:T(8,128)} fusion(f32[256,2048]{1,0:T(8,128)S(1)} %copy-done.13, f32[256,512]{1,0:T(8,128)S(1)} %fusion.1, f32[256,512]{1,0:T(8,128)S(1)} %fusion.2, f32[256,512]{1,0:T(8,128)S(1)} %fusion.3, f32[256,512]{1,0:T(8,128)S(1)} %fusion.4, f32[256,2048]{1,0:T(8,128)S(1)} %mul.1268, f32[2048]{0:T(1024)S(1)} %copy-done.16), kind=kLoop, calls=%fused_computation.1 | loop fusion | flops 3145728 | bytes 8396800 | tf_op jit(solution)/shard_map/mul | solution.py:165
  (118 shorter events, 18.8 us)
Async XLA Ops:
  6.5 75.9 %all-reduce.3.cloned.1.call-start = ((), (), s32[]{:S(2)}) async-start(), calls=%async_computation | async-start | bytes 1048576 | tf_op jit(solution)/shard_map/psum | solution.py:13
  8.3 4.6 %copy-start.17 = (s32[4]{0:T(128)S(1)}, s32[4]{0:T(128)}, u32[]{:S(2)}) copy-start(s32[4]{0:T(128)} %param.11) | copy-start | bytes 52
  8.3 27.8 %collective-permute-start = (f32[2,256,128]{2,1,0:T(8,128)}, f32[2,256,128]{2,1,0:T(8,128)}, u32[]{:S(2)}, u32[]{:S(2)}) collective-permute-start(f32[2,256,128]{2,1,0:T(8,128)} %get-tuple-element.112), channel_id=1, source_target_pairs={{0,1},{1,0},{2,3},{3,2},{4,5},{5,4},{6,7},{7,6},{8,9},{9,8},{10,11... | collective-permute-start | bytes 786440 | tf_op jit(solution)/shard_map/ppermute | solution.py:90
  10.9 77.5 %collective-permute-start.1 = (f32[256,2048]{1,0:T(8,128)S(1)}, f32[256,2048]{1,0:T(8,128)}, u32[]{:S(2)}, u32[]{:S(2)}) collective-permute-start(f32[256,2048]{1,0:T(8,128)S(1)} %mul.1268), channel_id=1, source_target_pairs={{0,4},{4,8},{1,5},{5,9},{2,6},{6,10},{3,7},{7,11},{16,20},{20,24},... | collective-permute-start | bytes 6291464 | tf_op jit(solution)/shard_map/ppermute | solution.py:129
  27.3 6.3 %copy-start.2 = (f32[512,256]{1,0:T(8,128)}, f32[512,256]{1,0:T(8,128)S(1)}, u32[]{:S(2)}) copy-start(f32[512,256]{1,0:T(8,128)S(1)} %fusion.92) | copy-start | bytes 1572868
  29.4 4.3 %copy-start.4 = (f32[512,256]{1,0:T(8,128)}, f32[512,256]{1,0:T(8,128)S(1)}, u32[]{:S(2)}) copy-start(f32[512,256]{1,0:T(8,128)S(1)} %fusion.94) | copy-start | bytes 1572868
  38.7 3.8 %copy-start.6 = (f32[512,256]{1,0:T(8,128)S(1)}, f32[512,256]{1,0:T(8,128)}, u32[]{:S(2)}) copy-start(f32[512,256]{1,0:T(8,128)} %fusion.84) | copy-start | bytes 1572868
  41.6 0.8 copy-start.8
  90.1 14.6 %collective-permute-start.2 = (f32[256,512]{1,0:T(8,128)S(1)}, f32[256,512]{1,0:T(8,128)S(1)}, u32[]{:S(2)}, u32[]{:S(2)}) collective-permute-start(f32[256,512]{1,0:T(8,128)S(1)} %get-tuple-element.65), channel_id=1, source_target_pairs={{4,8},{5,9},{6,10},{7,11},{20,24},{21,25},{22,26},{23,27}} | collective-permute-start | bytes 1572872 | tf_op jit(solution)/shard_map/ppermute | solution.py:146
  102.9 3.8 %copy-start.3 = (f32[512,256]{1,0:T(8,128)S(1)}, f32[512,256]{1,0:T(8,128)}, u32[]{:S(2)}) copy-start(f32[512,256]{1,0:T(8,128)} %copy-done.2) | copy-start | bytes 1572868
  102.9 3.8 %copy-start.5 = (f32[512,256]{1,0:T(8,128)S(1)}, f32[512,256]{1,0:T(8,128)}, u32[]{:S(2)}) copy-start(f32[512,256]{1,0:T(8,128)} %copy-done.4) | copy-start | bytes 1572868
  102.9 3.8 %copy-start.14 = (f32[512,256]{1,0:T(8,128)S(1)}, f32[512,256]{1,0:T(8,128)}, u32[]{:S(2)}) copy-start(f32[512,256]{1,0:T(8,128)} %fusion.96) | copy-start | bytes 1572868
  102.9 3.8 %copy-start.15 = (f32[512,256]{1,0:T(8,128)S(1)}, f32[512,256]{1,0:T(8,128)}, u32[]{:S(2)}) copy-start(f32[512,256]{1,0:T(8,128)} %fusion.98) | copy-start | bytes 1572868
  104.7 6.0 %collective-permute-start.4 = (f32[256,512]{1,0:T(8,128)S(1)}, f32[256,512]{1,0:T(8,128)S(1)}, u32[]{:S(2)}, u32[]{:S(2)}) collective-permute-start(f32[256,512]{1,0:T(8,128)S(1)} %get-tuple-element.28), channel_id=1, source_target_pairs={{4,8},{5,9},{6,10},{7,11},{20,24},{21,25},{22,26},{23,27}} | collective-permute-start | bytes 1572872 | tf_op jit(solution)/shard_map/ppermute | solution.py:146
  108.8 14.3 %collective-permute-start.3 = (f32[256,512]{1,0:T(8,128)S(1)}, f32[256,512]{1,0:T(8,128)S(1)}, u32[]{:S(2)}, u32[]{:S(2)}) collective-permute-start(f32[256,512]{1,0:T(8,128)S(1)} %convolution_add_fusion.6), channel_id=1, source_target_pairs={{8,12},{9,13},{10,14},{11,15},{24,28},{25,29},{26,30},{27,31}} | collective-permute-start | bytes 1572872 | tf_op jit(solution)/shard_map/ppermute | solution.py:161
  112.1 11.3 %copy-start.10 = (f32[2,512,256]{2,1,0:T(8,128)S(1)}, f32[2,512,256]{2,1,0:T(8,128)}, u32[]{:S(2)}) copy-start(f32[2,512,256]{2,1,0:T(8,128)} %pad_maximum_fusion) | copy-start | bytes 3145732
  124.0 3.1 %copy-start = (f32[512,256]{1,0:T(8,128)S(1)}, f32[512,256]{1,0:T(8,128)}, u32[]{:S(2)}) copy-start(f32[512,256]{1,0:T(8,128)} %fusion.88) | copy-start | bytes 1572868
  124.1 3.1 %copy-start.1 = (f32[512,256]{1,0:T(8,128)S(1)}, f32[512,256]{1,0:T(8,128)}, u32[]{:S(2)}) copy-start(f32[512,256]{1,0:T(8,128)} %fusion.90) | copy-start | bytes 1572868
  124.9 13.5 %collective-permute-start.5 = (f32[256,512]{1,0:T(8,128)S(1)}, f32[256,512]{1,0:T(8,128)S(1)}, u32[]{:S(2)}, u32[]{:S(2)}) collective-permute-start(f32[256,512]{1,0:T(8,128)S(1)} %convolution_add_fusion.4), channel_id=1, source_target_pairs={{8,12},{9,13},{10,14},{11,15},{24,28},{25,29},{26,30},{27,31}} | collective-permute-start | bytes 1572872 | tf_op jit(solution)/shard_map/ppermute | solution.py:161
  126.2 2.7 %collective-permute-start.6 = (f32[256,512]{1,0:T(8,128)S(1)}, f32[256,512]{1,0:T(8,128)S(1)}, u32[]{:S(2)}, u32[]{:S(2)}) collective-permute-start(f32[256,512]{1,0:T(8,128)S(1)} %get-tuple-element.33), channel_id=1, source_target_pairs={{4,8},{5,9},{6,10},{7,11},{20,24},{21,25},{22,26},{23,27}} | collective-permute-start | bytes 1572872 | tf_op jit(solution)/shard_map/ppermute | solution.py:146
  130.3 8.4 %copy-start.12 = (f32[2,512,256]{2,1,0:T(8,128)S(1)}, f32[2,512,256]{2,1,0:T(8,128)}, u32[]{:S(2)}) copy-start(f32[2,512,256]{2,1,0:T(8,128)} %pad_maximum_fusion.3) | copy-start | bytes 3145732
  139.9 3.1 %collective-permute-start.8 = (f32[256,512]{1,0:T(8,128)S(1)}, f32[256,512]{1,0:T(8,128)S(1)}, u32[]{:S(2)}, u32[]{:S(2)}) collective-permute-start(f32[256,512]{1,0:T(8,128)S(1)} %get-tuple-element.38), channel_id=1, source_target_pairs={{4,8},{5,9},{6,10},{7,11},{20,24},{21,25},{22,26},{23,27}} | collective-permute-start | bytes 1572872 | tf_op jit(solution)/shard_map/ppermute | solution.py:146
  141.0 3.2 %copy-start.7 = (f32[512,256]{1,0:T(8,128)S(1)}, f32[512,256]{1,0:T(8,128)}, u32[]{:S(2)}) copy-start(f32[512,256]{1,0:T(8,128)} %fusion.84) | copy-start | bytes 1572868
  141.0 3.2 %copy-start.9 = (f32[512,256]{1,0:T(8,128)S(1)}, f32[512,256]{1,0:T(8,128)}, u32[]{:S(2)}) copy-start(f32[512,256]{1,0:T(8,128)} %copy-done.8) | copy-start | bytes 1572868
  141.0 16.7 %collective-permute-start.7 = (f32[256,512]{1,0:T(8,128)S(1)}, f32[256,512]{1,0:T(8,128)S(1)}, u32[]{:S(2)}, u32[]{:S(2)}) collective-permute-start(f32[256,512]{1,0:T(8,128)S(1)} %convolution_add_fusion.2), channel_id=1, source_target_pairs={{8,12},{9,13},{10,14},{11,15},{24,28},{25,29},{26,30},{27,31}} | collective-permute-start | bytes 1572872 | tf_op jit(solution)/shard_map/ppermute | solution.py:161
  145.2 12.8 %copy-start.11 = (f32[2,512,256]{2,1,0:T(8,128)S(1)}, f32[2,512,256]{2,1,0:T(8,128)}, u32[]{:S(2)}) copy-start(f32[2,512,256]{2,1,0:T(8,128)} %pad_maximum_fusion.6) | copy-start | bytes 3145732
  159.5 12.8 %collective-permute-start.9 = (f32[256,512]{1,0:T(8,128)S(1)}, f32[256,512]{1,0:T(8,128)S(1)}, u32[]{:S(2)}, u32[]{:S(2)}) collective-permute-start(f32[256,512]{1,0:T(8,128)S(1)} %convolution_add_fusion), channel_id=1, source_target_pairs={{8,12},{9,13},{10,14},{11,15},{24,28},{25,29},{26,30},{27,31}} | collective-permute-start | bytes 1572872 | tf_op jit(solution)/shard_map/ppermute | solution.py:161
  161.4 11.3 %copy-start.13 = (f32[256,2048]{1,0:T(8,128)S(1)}, f32[256,2048]{1,0:T(8,128)}, u32[]{:S(2)}) copy-start(f32[256,2048]{1,0:T(8,128)} %param.6) | copy-start | bytes 6291460
  161.4 11.3 %copy-start.16 = (f32[2048]{0:T(1024)S(1)}, f32[2048]{0:T(1024)}, u32[]{:S(2)}) copy-start(f32[2048]{0:T(1024)} %param.9) | copy-start | bytes 24580
Sparse Core Ops, SparseCore 0:
  38.8 43.5 all-reduce.2
where the time goes:
time: 183 us; the launch traced here: 181 us
  waiting for transfers between devices  80.6 us (44%)
  matrix products  36.2 us (20%)
  between operations  24.4 us (13%)
  other arithmetic  20.4 us (11%)
  starting transfers between devices  10.5 us (6%)
  local copies, waits for them, and re-layouts  9.42 us (5%)
    ppermute x4, waiting for transfers between devices, body(): sent = lax.ppermute(partial, 'ctx', [(last_raw, last_raw + 1)])  41.6 us
    psum x1, waiting for transfers between devices, from_root(): return lax.psum(block, axis)  38.9 us
    dot_general x12, matrix products, transform_rows(): jnp.einsum('pc,fp->cf', block, fwd_imag, precision=DATA_PRECISION)  14 us
    dot_general x12, matrix products, transform_rows(): jnp.einsum('pc,fp->cf', block, fwd_real, precision=DATA_PRECISION)  13.3 us
    ppermute x4, starting transfers between devices, body(): sent = lax.ppermute(partial, 'ctx', [(last_raw, last_raw + 1)])  5.3 us
    another operation x9, other arithmetic, transform_rows(): jnp.stack([jnp.einsum('pc,fp->cf', block, fwd_real, precision=DATA_PRECIS...  4.79 us
    select_n x6, other arithmetic, apply_filter(): jnp.where(first_col, a_real * e_real, a_real * e_real - a_imag * e_imag)  3.67 us
  transfers between devices with their start and end apart: 11, of which 5 were waited for; matrix products, arithmetic and copies ran while one was open for 30% of the time, Pallas kernels for 0%

commit v1 on v0

--- a/solution.py
+++ b/solution.py
@@ -92,6 +92,8 @@
             )
         received.append(wanted)
     received = jnp.stack(received)
+    key_in, values_in, received = lax.optimization_barrier((key_in, values_in, received))
+    mixed_input = key_in * values_in
     pieces = []
     for cycle_step in range(cycle_steps):
         slot_index = lag_slot[cycle_step]

time: 183 us -> 191 us (1.044)
  waiting for transfers between devices: 80.6 us -> 90.8 us
    ppermute x4, waiting for transfers between devices: 41.6 us -> 48 us  [body(): sent = lax.ppermute(partial, 'ctx', [(last_raw, last_raw + 1)])]
    psum x1, waiting for transfers between devices: 38.9 us -> 42.7 us  [from_root(): return lax.psum(block, axis)]
  transfers between devices with their start and end apart: 11 -> 11, of which waited for: 5 -> 5; matrix products, arithmetic and copies ran while one was open for 30% -> 27% of each run, Pallas kernels for 0% -> 0%
where the time goes in v1:
time: 191 us; the launch traced here: 190 us
  waiting for transfers between devices  90.8 us (48%)
  matrix products  36.2 us (19%)
  between operations  24.6 us (13%)
  other arithmetic  18.9 us (10%)
  starting transfers between devices  10.6 us (6%)
  local copies, waits for them, and re-layouts  8.71 us (5%)
    ppermute x4, waiting for transfers between devices, body(): sent = lax.ppermute(partial, 'ctx', [(last_raw, last_raw + 1)])  48 us
    psum x1, waiting for transfers between devices, from_root(): return lax.psum(block, axis)  42.7 us
    dot_general x12, matrix products, transform_rows(): jnp.einsum('pc,fp->cf', block, fwd_real, precision=DATA_PRECISION)  14.1 us
    dot_general x12, matrix products, transform_rows(): jnp.einsum('pc,fp->cf', block, fwd_imag, precision=DATA_PRECISION)  13.2 us
    ppermute x4, starting transfers between devices, body(): sent = lax.ppermute(partial, 'ctx', [(last_raw, last_raw + 1)])  5.3 us
    another operation x9, other arithmetic, transform_rows(): jnp.stack([jnp.einsum('pc,fp->cf', block, fwd_real, precision=DATA_PRECIS...  4.94 us
  transfers between devices with their start and end apart: 11, of which 5 were waited for; matrix products, arithmetic and copies ran while one was open for 27% of the time, Pallas kernels for 0%

profile of v1, /device:TPU:24, one launch (start us, length us, event | category | flops | bytes accessed | tf_op | source)
XLA Modules:
  0.0 189.8 jit_solution(10193263384579061743)
XLA Ops:
  6.5 1.1 dynamic-slice_bitcast_fusion
  7.7 2.1 %select_multiply_fusion = (f32[256,256]{1,0:T(8,128)S(1)}, f32[256,256]{1,0:T(8,128)S(1)}, f32[256,256]{1,0:T(8,128)S(1)}) fusion(s32[256]{0:T(256)S(1)} %get-tuple-element.194, s32[256]{0:T(256)S(1)} %get-tuple-element.195, s32[256]{0:T(256)S(1)} %get-tuple-element.198, pred[256]{0:T(512)(128)(4,1)S(1)} %get-tuple-element.196, ...), kind=kLoop, calls=%fused_computation.292 | loop fusion | flops 2883584 | bytes 792320 | tf_op jit(solution)/shard_map/div | solution.py:27
  9.9 1.5 fusion.137
  21.5 1.0 fusion.117
  22.6 2.5 %mul.1270 = f32[256,2048]{1,0:T(8,128)S(1)} multiply(f32[256,2048]{1,0:T(8,128)} %param.7, f32[256,2048]{1,0:T(8,128)} %param.8) | non-fusion elementwise | flops 524288 | bytes 6291456 | tf_op jit(solution)/shard_map/mul | solution.py:96
  25.0 2.0 %collective-permute-start.1 = (f32[256,2048]{1,0:T(8,128)S(1)}, f32[256,2048]{1,0:T(8,128)}, u32[]{:S(2)}, u32[]{:S(2)}) collective-permute-start(f32[256,2048]{1,0:T(8,128)S(1)} %mul.1270), channel_id=1, source_target_pairs={{0,4},{4,8},{1,5},{5,9},{2,6},{6,10},{3,7},{7,11},{16,20},{20,24},... | collective-permute-start | bytes 6291464 | tf_op jit(solution)/shard_map/ppermute | solution.py:131
  27.7 1.4 fusion.96
  29.7 1.4 fusion.98
  31.1 1.4 fusion.88
  32.6 1.4 fusion.90
  34.0 1.4 fusion.86
  35.4 1.0 pad_maximum_fusion
  36.5 0.8 select_bitcast_fusion
  38.0 2.4 %pad_maximum_fusion.3 = f32[2,512,256]{2,1,0:T(8,128)} fusion(f32[1,512,256]{2,1,0:T(8,128)} %bitcast.682, f32[1,512,256]{2,1,0:T(8,128)} %bitcast.683), kind=kLoop, calls=%fused_computation.51 | loop fusion | flops 262144 | bytes 2097152 | tf_op jit(solution)/shard_map/stack | solution.py:38
  40.4 1.0 pad_maximum_fusion.6
  41.4 42.7 %all-reduce.3.cloned.1.call-done = (f32[256,128]{1,0:T(8,128)}, f32[256,128]{1,0:T(8,128)}, f32[256,128]{1,0:T(8,128)}, f32[256,128]{1,0:T(8,128)}) async-done(((f32[256,128]{1,0:T(8,128)}, f32[256,128]{1,0:T(8,128)}, f32[256,128]{1,0:T(8,128)}, f32[256,128]{1,0:T(8,128)}), (f32[256,128]{1,0:T(8,128)}, f32[256,128]{1,0:T(8,128)}, f32[256,128]{1,0:T(8,128)}, ...) | async-done | bytes 524304 | tf_op jit(solution)/shard_map/psum | solution.py:13
  84.2 0.9 constant_dynamic-update-slice_fusion.3
  85.1 0.9 constant_dynamic-update-slice_fusion.2
  86.0 0.9 constant_dynamic-update-slice_fusion.1
  86.9 0.9 constant_dynamic-update-slice_fusion
  87.8 1.0 convolution_bitcast_fusion.1
  88.9 1.0 convolution_bitcast_fusion
  90.2 1.7 fusion.136
  91.9 0.9 collective-permute-start.2
  92.8 1.7 fusion.128
  94.4 1.7 fusion.130
  96.2 1.7 fusion.124
  97.8 1.7 fusion.126
  99.6 1.7 fusion.120
  101.2 1.7 fusion.122
  103.0 1.7 fusion.132
  104.7 1.8 fusion.134
  106.5 0.7 collective-permute-start.4
  108.5 1.0 fusion.13
  110.5 1.3 collective-permute-start.3
  112.5 0.6 fusion.140
  113.8 13.9 %collective-permute-done.3 = f32[256,512]{1,0:T(8,128)S(1)} collective-permute-done((f32[256,512]{1,0:T(8,128)S(1)}, f32[256,512]{1,0:T(8,128)S(1)}, u32[]{:S(2)}, u32[]{:S(2)}) %collective-permute-start.3) | collective-permute-done | bytes 524320 | tf_op jit(solution)/shard_map/ppermute | solution.py:163
  129.7 1.3 collective-permute-start.5
  131.0 0.9 collective-permute-start.6
  131.9 0.7 fusion.21
  135.1 9.3 %collective-permute-done.5 = f32[256,512]{1,0:T(8,128)S(1)} collective-permute-done((f32[256,512]{1,0:T(8,128)S(1)}, f32[256,512]{1,0:T(8,128)S(1)}, u32[]{:S(2)}, u32[]{:S(2)}) %collective-permute-start.5) | collective-permute-done | bytes 524320 | tf_op jit(solution)/shard_map/ppermute | solution.py:163
  145.8 0.7 collective-permute-start.8
  147.0 1.4 collective-permute-start.7
  150.1 0.7 fusion.24
  151.5 13.3 %collective-permute-done.7 = f32[256,512]{1,0:T(8,128)S(1)} collective-permute-done((f32[256,512]{1,0:T(8,128)S(1)}, f32[256,512]{1,0:T(8,128)S(1)}, u32[]{:S(2)}, u32[]{:S(2)}) %collective-permute-start.7) | collective-permute-done | bytes 524320 | tf_op jit(solution)/shard_map/ppermute | solution.py:163
  166.6 1.3 collective-permute-start.9
  169.0 11.6 %collective-permute-done.9 = f32[256,512]{1,0:T(8,128)S(1)} collective-permute-done((f32[256,512]{1,0:T(8,128)S(1)}, f32[256,512]{1,0:T(8,128)S(1)}, u32[]{:S(2)}, u32[]{:S(2)}) %collective-permute-start.9) | collective-permute-done | bytes 524320 | tf_op jit(solution)/shard_map/ppermute | solution.py:163
  181.1 1.9 %fusion = f32[256,2048]{1,0:T(8,128)} fusion(f32[256,2048]{1,0:T(8,128)S(1)} %copy-done.13, f32[256,512]{1,0:T(8,128)S(1)} %fusion.1, f32[256,512]{1,0:T(8,128)S(1)} %fusion.2, f32[256,512]{1,0:T(8,128)S(1)} %fusion.3, f32[256,512]{1,0:T(8,128)S(1)} %fusion.4, f32[256,2048]{1,0:T(8,128)S(1)} %mul.1270, f32[2048]{0:T(1024)S(1)} %copy-done.16), kind=kLoop, calls=%fused_computation.1 | loop fusion | flops 3145728 | bytes 8396800 | tf_op jit(solution)/shard_map/mul | solution.py:167
  (116 shorter events, 17.7 us)
Async XLA Ops:
  6.5 77.6 %all-reduce.3.cloned.1.call-start = ((), (), s32[]{:S(2)}) async-start(), calls=%async_computation | async-start | bytes 1048576 | tf_op jit(solution)/shard_map/psum | solution.py:13
  7.6 14.9 %collective-permute-start = (f32[2,256,128]{2,1,0:T(8,128)S(1)}, f32[2,256,128]{2,1,0:T(8,128)S(1)}, u32[]{:S(2)}, u32[]{:S(2)}) collective-permute-start(f32[2,256,128]{2,1,0:T(8,128)S(1)} %get-tuple-element.120), channel_id=1, source_target_pairs={{0,1},{1,0},{2,3},{3,2},{4,5},{5,4},{6,7},{7,6},{8,9},{9,8},{10,11... | collective-permute-start | bytes 786440 | tf_op jit(solution)/shard_map/ppermute | solution.py:90
  25.0 65.1 %collective-permute-start.1 = (f32[256,2048]{1,0:T(8,128)S(1)}, f32[256,2048]{1,0:T(8,128)}, u32[]{:S(2)}, u32[]{:S(2)}) collective-permute-start(f32[256,2048]{1,0:T(8,128)S(1)} %mul.1270), channel_id=1, source_target_pairs={{0,4},{4,8},{1,5},{5,9},{2,6},{6,10},{3,7},{7,11},{16,20},{20,24},... | collective-permute-start | bytes 6291464 | tf_op jit(solution)/shard_map/ppermute | solution.py:131
  27.7 7.8 %copy-start.6 = (f32[512,256]{1,0:T(8,128)}, f32[512,256]{1,0:T(8,128)S(1)}, u32[]{:S(2)}) copy-start(f32[512,256]{1,0:T(8,128)S(1)} %fusion.92) | copy-start | bytes 1572868
  29.7 5.7 %copy-start.8 = (f32[512,256]{1,0:T(8,128)}, f32[512,256]{1,0:T(8,128)S(1)}, u32[]{:S(2)}) copy-start(f32[512,256]{1,0:T(8,128)S(1)} %fusion.94) | copy-start | bytes 1572868
  37.3 3.1 %copy-start = (f32[512,256]{1,0:T(8,128)S(1)}, f32[512,256]{1,0:T(8,128)}, u32[]{:S(2)}) copy-start(f32[512,256]{1,0:T(8,128)} %fusion.86) | copy-start | bytes 1572868
  38.0 2.4 %copy-start.2 = (f32[512,256]{1,0:T(8,128)}, f32[512,256]{1,0:T(8,128)S(1)}, u32[]{:S(2)}) copy-start(f32[512,256]{1,0:T(8,128)S(1)} %fusion.84) | copy-start | bytes 1572868
  91.9 14.6 %collective-permute-start.2 = (f32[256,512]{1,0:T(8,128)S(1)}, f32[256,512]{1,0:T(8,128)S(1)}, u32[]{:S(2)}, u32[]{:S(2)}) collective-permute-start(f32[256,512]{1,0:T(8,128)S(1)} %get-tuple-element.71), channel_id=1, source_target_pairs={{4,8},{5,9},{6,10},{7,11},{20,24},{21,25},{22,26},{23,27}} | collective-permute-start | bytes 1572872 | tf_op jit(solution)/shard_map/ppermute | solution.py:148
  104.6 3.8 %copy-start.7 = (f32[512,256]{1,0:T(8,128)S(1)}, f32[512,256]{1,0:T(8,128)}, u32[]{:S(2)}) copy-start(f32[512,256]{1,0:T(8,128)} %copy-done.6) | copy-start | bytes 1572868
  104.6 3.8 %copy-start.9 = (f32[512,256]{1,0:T(8,128)S(1)}, f32[512,256]{1,0:T(8,128)}, u32[]{:S(2)}) copy-start(f32[512,256]{1,0:T(8,128)} %copy-done.8) | copy-start | bytes 1572868
  104.7 3.8 %copy-start.14 = (f32[512,256]{1,0:T(8,128)S(1)}, f32[512,256]{1,0:T(8,128)}, u32[]{:S(2)}) copy-start(f32[512,256]{1,0:T(8,128)} %fusion.96) | copy-start | bytes 1572868
  104.7 3.8 %copy-start.15 = (f32[512,256]{1,0:T(8,128)S(1)}, f32[512,256]{1,0:T(8,128)}, u32[]{:S(2)}) copy-start(f32[512,256]{1,0:T(8,128)} %fusion.98) | copy-start | bytes 1572868
  106.5 6.0 %collective-permute-start.4 = (f32[256,512]{1,0:T(8,128)S(1)}, f32[256,512]{1,0:T(8,128)S(1)}, u32[]{:S(2)}, u32[]{:S(2)}) collective-permute-start(f32[256,512]{1,0:T(8,128)S(1)} %get-tuple-element.34), channel_id=1, source_target_pairs={{4,8},{5,9},{6,10},{7,11},{20,24},{21,25},{22,26},{23,27}} | collective-permute-start | bytes 1572872 | tf_op jit(solution)/shard_map/ppermute | solution.py:148
  110.5 17.2 %collective-permute-start.3 = (f32[256,512]{1,0:T(8,128)S(1)}, f32[256,512]{1,0:T(8,128)S(1)}, u32[]{:S(2)}, u32[]{:S(2)}) collective-permute-start(f32[256,512]{1,0:T(8,128)S(1)} %convolution_add_fusion.6), channel_id=1, source_target_pairs={{8,12},{9,13},{10,14},{11,15},{24,28},{25,29},{26,30},{27,31}} | collective-permute-start | bytes 1572872 | tf_op jit(solution)/shard_map/ppermute | solution.py:163
  113.8 14.2 %copy-start.12 = (f32[2,512,256]{2,1,0:T(8,128)S(1)}, f32[2,512,256]{2,1,0:T(8,128)}, u32[]{:S(2)}) copy-start(f32[2,512,256]{2,1,0:T(8,128)} %pad_maximum_fusion) | copy-start | bytes 3145732
  128.8 3.1 %copy-start.4 = (f32[512,256]{1,0:T(8,128)S(1)}, f32[512,256]{1,0:T(8,128)}, u32[]{:S(2)}) copy-start(f32[512,256]{1,0:T(8,128)} %fusion.88) | copy-start | bytes 1572868
  128.8 3.1 %copy-start.5 = (f32[512,256]{1,0:T(8,128)S(1)}, f32[512,256]{1,0:T(8,128)}, u32[]{:S(2)}) copy-start(f32[512,256]{1,0:T(8,128)} %fusion.90) | copy-start | bytes 1572868
  129.7 14.7 %collective-permute-start.5 = (f32[256,512]{1,0:T(8,128)S(1)}, f32[256,512]{1,0:T(8,128)S(1)}, u32[]{:S(2)}, u32[]{:S(2)}) collective-permute-start(f32[256,512]{1,0:T(8,128)S(1)} %convolution_add_fusion.4), channel_id=1, source_target_pairs={{8,12},{9,13},{10,14},{11,15},{24,28},{25,29},{26,30},{27,31}} | collective-permute-start | bytes 1572872 | tf_op jit(solution)/shard_map/ppermute | solution.py:163
  131.0 2.7 %collective-permute-start.6 = (f32[256,512]{1,0:T(8,128)S(1)}, f32[256,512]{1,0:T(8,128)S(1)}, u32[]{:S(2)}, u32[]{:S(2)}) collective-permute-start(f32[256,512]{1,0:T(8,128)S(1)} %get-tuple-element.39), channel_id=1, source_target_pairs={{4,8},{5,9},{6,10},{7,11},{20,24},{21,25},{22,26},{23,27}} | collective-permute-start | bytes 1572872 | tf_op jit(solution)/shard_map/ppermute | solution.py:148
  135.1 9.5 %copy-start.11 = (f32[2,512,256]{2,1,0:T(8,128)S(1)}, f32[2,512,256]{2,1,0:T(8,128)}, u32[]{:S(2)}) copy-start(f32[2,512,256]{2,1,0:T(8,128)} %pad_maximum_fusion.3) | copy-start | bytes 3145732
  145.8 3.0 %collective-permute-start.8 = (f32[256,512]{1,0:T(8,128)S(1)}, f32[256,512]{1,0:T(8,128)S(1)}, u32[]{:S(2)}, u32[]{:S(2)}) collective-permute-start(f32[256,512]{1,0:T(8,128)S(1)} %get-tuple-element.44), channel_id=1, source_target_pairs={{4,8},{5,9},{6,10},{7,11},{20,24},{21,25},{22,26},{23,27}} | collective-permute-start | bytes 1572872 | tf_op jit(solution)/shard_map/ppermute | solution.py:148
  146.9 3.1 %copy-start.1 = (f32[512,256]{1,0:T(8,128)S(1)}, f32[512,256]{1,0:T(8,128)}, u32[]{:S(2)}) copy-start(f32[512,256]{1,0:T(8,128)} %fusion.86) | copy-start | bytes 1572868
  146.9 3.1 %copy-start.3 = (f32[512,256]{1,0:T(8,128)S(1)}, f32[512,256]{1,0:T(8,128)}, u32[]{:S(2)}) copy-start(f32[512,256]{1,0:T(8,128)} %copy-done.2) | copy-start | bytes 1572868
  147.0 17.9 %collective-permute-start.7 = (f32[256,512]{1,0:T(8,128)S(1)}, f32[256,512]{1,0:T(8,128)S(1)}, u32[]{:S(2)}, u32[]{:S(2)}) collective-permute-start(f32[256,512]{1,0:T(8,128)S(1)} %convolution_add_fusion.2), channel_id=1, source_target_pairs={{8,12},{9,13},{10,14},{11,15},{24,28},{25,29},{26,30},{27,31}} | collective-permute-start | bytes 1572872 | tf_op jit(solution)/shard_map/ppermute | solution.py:163
  151.1 14.0 %copy-start.10 = (f32[2,512,256]{2,1,0:T(8,128)S(1)}, f32[2,512,256]{2,1,0:T(8,128)}, u32[]{:S(2)}) copy-start(f32[2,512,256]{2,1,0:T(8,128)} %pad_maximum_fusion.6) | copy-start | bytes 3145732
  166.6 14.0 %collective-permute-start.9 = (f32[256,512]{1,0:T(8,128)S(1)}, f32[256,512]{1,0:T(8,128)S(1)}, u32[]{:S(2)}, u32[]{:S(2)}) collective-permute-start(f32[256,512]{1,0:T(8,128)S(1)} %convolution_add_fusion), channel_id=1, source_target_pairs={{8,12},{9,13},{10,14},{11,15},{24,28},{25,29},{26,30},{27,31}} | collective-permute-start | bytes 1572872 | tf_op jit(solution)/shard_map/ppermute | solution.py:163
  168.6 12.5 %copy-start.13 = (f32[256,2048]{1,0:T(8,128)S(1)}, f32[256,2048]{1,0:T(8,128)}, u32[]{:S(2)}) copy-start(f32[256,2048]{1,0:T(8,128)} %param.6) | copy-start | bytes 6291460
  168.6 12.5 %copy-start.16 = (f32[2048]{0:T(1024)S(1)}, f32[2048]{0:T(1024)}, u32[]{:S(2)}) copy-start(f32[2048]{0:T(1024)} %param.9) | copy-start | bytes 24580
Sparse Core Ops, SparseCore 0:
  37.4 46.6 all-reduce.2
